TPU v7x, 256 devices: a whole 4x4x8 slice. The times are simulated.
256 devices in a mesh: section: 4 (over x_hi, core), expert: 4 (over y), dp: 16 (over z, x_lo).
Axes of the slice: x: 4 (x_hi: 2, x_lo: 2; x = x_hi * 2 + x_lo), y: 4, z: 8, core: 2. Of those that a mesh axis runs over, the one named last changes fastest.
Arguments:
- tokens: bfloat16 [2, 4096, 3072], P(None, ('expert', 'dp')), may hold values from -6 to 6
- routes: int32 [2, 4096, 2], P(None, ('expert', 'dp')), may hold values from 0 to 3, all different within a row; in each aligned block of 64 rows (0 to 63, 64 to 127, ..., all dimensions but the last counted through in order) at most 36 rows name the same one
- router: bfloat16 [3072, 4], replicated, may hold values from -0.109375 to 0.109375
- gate_weight: bfloat16 [4, 8192, 3072], P('expert', ('section', 'dp')), may hold values from -0.109375 to 0.109375
- up_weight: bfloat16 [4, 8192, 3072], P('expert', ('section', 'dp')), may hold values from -0.109375 to 0.109375
- down_weight: bfloat16 [4, 8192, 3072], P('expert', ('section', 'dp')), may hold values from -0.0625 to 0.0625
Outputs:
- activations: bfloat16 [2, 4096, 3072], P(None, ('expert', 'dp'), 'section')
- gram: bfloat16 [4, 3072, 3072], P('expert', ('section', 'dp'))
Inputs may be any that keep to these rules, and one draw needn't show every extreme that they name: `routes`: in every micro-batch, each aligned block of 64 tokens (the tokens of one device) names no expert more than 36 times, a bound that some block reaches; the two experts of a token differ; every expert is named somewhere.
All inputs are finite; a program needn't handle non-finite values.
Results may differ from a plain program's by a relative error of at most 0.02.
Values may be sent and summed in bfloat16 or wider, within the bound.
No kernel may reach another device: no remote copies, remote signals or barrier semaphores. Data moves between devices by JAX's collectives and lax.ppermute only.
A program may use at most 128 MiB of HBM per device.

v0:
```python
import jax
import jax.numpy as jnp
from jax import lax
from jax.sharding import PartitionSpec as P


def route_targets(route_ids, experts, capacity):
    onehot = (route_ids[:, :, None] == jnp.arange(experts, dtype=jnp.int32)[None, None, :]).astype(
        jnp.int32
    )
    flattened = onehot.reshape(-1, experts)
    before = jnp.cumsum(flattened, axis=0) - flattened
    slot_rank = jnp.sum(before * flattened, axis=1).reshape(route_ids.shape)
    return route_ids * capacity + slot_rank


def on_device(tokens, routes, router, gate_weight, up_weight, down_weight):
    micro_count = tokens.shape[0]
    rows_dev = tokens.shape[1]
    model_width = tokens.shape[2]
    experts = router.shape[1]
    capacity = 9 * rows_dev // (4 * experts)
    section_count = lax.axis_size("section")
    replicas = lax.axis_size("dp")
    section_index = lax.axis_index("section")
    col_width = model_width // section_count
    gate_rows = gate_weight[0]
    up_rows = up_weight[0]
    down_rows = down_weight[0]
    logits = jnp.einsum("mtd,de->mte", tokens, router, preferred_element_type=jnp.float32)
    chosen = jnp.take_along_axis(logits, routes, axis=-1)
    logit_gap = chosen[..., 0] - chosen[..., 1]
    first_gate = jax.nn.sigmoid(logit_gap)
    second_gate = jax.nn.sigmoid(-logit_gap)
    target = jax.vmap(lambda one_block: route_targets(one_block, experts, capacity))(routes)
    slot_ids = jnp.arange(experts * capacity, dtype=jnp.int32)
    placing = jnp.sum(
        (slot_ids[None, :, None, None] == target[:, None, :, :]).astype(jnp.float32), axis=3
    ).astype(jnp.bfloat16)
    outgoing = jnp.einsum(
        "mst,mtd->msd", placing, tokens, preferred_element_type=jnp.float32
    ).astype(jnp.bfloat16)
    outgoing = outgoing.reshape(micro_count, experts, capacity, model_width)
    arrived = lax.all_to_all(outgoing, "expert", split_axis=1, concat_axis=1, tiled=True)
    rows_all = arrived.reshape(-1, model_width)
    gate_piece = lax.all_gather(gate_rows, "dp", axis=0, tiled=True)
    up_piece = lax.all_gather(up_rows, "dp", axis=0, tiled=True)
    down_piece = lax.all_gather(down_rows, "dp", axis=0, tiled=True)
    gate_part = lax.dot_general(
        rows_all, gate_piece, (((1,), (1,)), ((), ())), preferred_element_type=jnp.float32
    )
    up_part = lax.dot_general(
        rows_all, up_piece, (((1,), (1,)), ((), ())), preferred_element_type=jnp.float32
    )
    inner_units = (jax.nn.silu(gate_part) * up_part).astype(jnp.bfloat16)
    partial_out = jnp.dot(inner_units, down_piece, preferred_element_type=jnp.float32)
    summed_out = lax.psum_scatter(
        partial_out.astype(jnp.bfloat16), "section", scatter_dimension=1, tiled=True
    )
    expert_out = summed_out.reshape(micro_count, experts, capacity, col_width)
    returned = lax.all_to_all(expert_out, "expert", split_axis=1, concat_axis=1, tiled=True)
    flat_back = returned.reshape(micro_count, experts * capacity, col_width)
    first_rows = jnp.take_along_axis(flat_back, target[:, :, 0][:, :, None], axis=1).astype(
        jnp.float32
    )
    second_rows = jnp.take_along_axis(flat_back, target[:, :, 1][:, :, None], axis=1).astype(
        jnp.float32
    )
    own_cols = lax.dynamic_slice_in_dim(tokens, section_index * col_width, col_width, 2).astype(
        jnp.float32
    )
    layer_out = (
        own_cols + first_gate[..., None] * first_rows + second_gate[..., None] * second_rows
    ).astype(jnp.bfloat16)
    all_tokens = rows_dev * lax.axis_size("expert") * replicas
    gram_scale = experts / (2.0 * micro_count * all_tokens)
    block_rows = col_width // replicas
    left_cols = lax.dynamic_slice_in_dim(
        rows_all, section_index * col_width, block_rows * lax.axis_size("dp"), 1
    )
    product = (
        lax.dot_general(
            left_cols, rows_all, (((0,), (0,)), ((), ())), preferred_element_type=jnp.float32
        )
        * gram_scale
    )
    rounded = lax.optimization_barrier(product.astype(jnp.bfloat16))
    gram_block = lax.psum_scatter(
        rounded.astype(jnp.float32).astype(jnp.bfloat16), "dp", scatter_dimension=0, tiled=True
    )
    return (layer_out, gram_block[None])


def solution(mesh):
    return jax.shard_map(
        on_device,
        mesh=mesh,
        in_specs=(
            P(None, ("expert", "dp"), None),
            P(None, ("expert", "dp"), None),
            P(),
            P("expert", ("section", "dp"), None),
            P("expert", ("section", "dp"), None),
            P("expert", ("section", "dp"), None),
        ),
        out_specs=(P(None, ("expert", "dp"), "section"), P("expert", ("section", "dp"), None)),
        check_vma=False,
    )
```

profile of v0, /device:TPU:50, one launch (start us, length us, event | category | flops | bytes accessed | tf_op | source)
XLA Modules:
  0.0 997.7 jit_solution(10317960741379310035)
XLA Ops:
  7.2 0.0 copy-start
  7.2 0.0 copy-start.3
  7.2 0.0 copy-start.1
  7.2 0.0 all-gather.7.cloned.1.call-start
  7.2 0.7 all-gather.7.cloned.1.call-update
  7.9 0.0 all-gather.11.cloned.1.call-start
  8.0 0.7 all-gather.11.cloned.1.call-update
  8.7 0.0 all-gather.9.cloned.1.call-start
  8.7 0.7 all-gather.9.cloned.1.call-update
  9.4 0.0 reduce-scatter.3.cloned.1.call-start
  9.5 0.0 copy-done.3
  9.5 0.1 copy.68
  9.6 0.1 eq.30
  9.7 0.1 fusion.18
  9.8 0.2 reduce_window_sum.11
  10.0 0.2 select_reduce_fusion
  10.2 0.1 reshape.35
  10.4 0.1 copy.69
  10.5 0.1 convert_reduce_fusion
  10.6 0.0 copy-done.1
  10.6 0.7 convolution_convert_fusion
  11.2 1.8 copy.70
  13.1 24.9 %all_to_all.10 = bf16[2,4,36,3072]{3,0,2,1:T(2,128)(2,1)S(1)} all-to-all(bf16[2,4,36,3072]{3,0,2,1:T(2,128)(2,1)S(1)} %bitcast.45), channel_id=1, replica_groups=mesh['section'=4,'expert'=4,'dp'=16] {'expert'}, dimensions={1} | all-to-all | bytes 3538944 | tf_op jit(solution)/shard_map/all_to_all | solution.py:44
  38.0 0.4 copy.71
  38.4 1.4 reshape.37
  39.8 0.0 copy-start.2
  39.8 243.2 %all-gather.7.cloned.1.call-done = bf16[1,2048,3072]{2,1,0:T(8,128)(2,1)} async-done(((bf16[1,128,3072]{2,1,0:T(8,128)(2,1)}), bf16[1,2048,3072]{2,1,0:T(8,128)(2,1)}) %all-gather.7.cloned.1.call-update) | async-done | bytes 12582928 | tf_op jit(solution)/shard_map/all_gather | solution.py:46
  283.0 10.4 %fusion.4 = f32[288,2048]{1,0:T(8,128)} fusion(bf16[288,3072]{1,0:T(8,128)(2,1)} %reshape.37, bf16[1,2048,3072]{2,1,0:T(8,128)(2,1)} %all-gather.7.cloned.1.call-done), kind=kOutput, calls=%fused_computation.7 | convolution fusion | flops 3623878656 | bytes 16711680 | tf_op jit(solution)/shard_map/dot_general | solution.py:49
  293.4 260.4 %all-gather.11.cloned.1.call-done = bf16[1,2048,3072]{2,1,0:T(8,128)(2,1)} async-done(((bf16[1,128,3072]{2,1,0:T(8,128)(2,1)}), bf16[1,2048,3072]{2,1,0:T(8,128)(2,1)}) %all-gather.11.cloned.1.call-update) | async-done | bytes 12582928 | tf_op jit(solution)/shard_map/all_gather | solution.py:48
  553.7 270.7 %all-gather.9.cloned.1.call-done = bf16[1,2048,3072]{2,1,0:T(8,128)(2,1)} async-done(((bf16[1,128,3072]{2,1,0:T(8,128)(2,1)}), bf16[1,2048,3072]{2,1,0:T(8,128)(2,1)}) %all-gather.9.cloned.1.call-update) | async-done | bytes 12582928 | tf_op jit(solution)/shard_map/all_gather | solution.py:47
  824.5 0.0 copy-done.2
  824.5 14.5 %fusion.6 = bf16[288,3072]{1,0:T(8,128)(2,1)} fusion(bf16[1,2048,3072]{2,1,0:T(8,128)(2,1)} %all-gather.11.cloned.1.call-done, bf16[288,3072]{1,0:T(8,128)(2,1)S(1)} %copy-done.2, bf16[1,2048,3072]{2,1,0:T(8,128)(2,1)} %all-gather.9.cloned.1.call-done, f32[288,2048]{1,0:T(8,128)} %fusion.4), kind=kOutput, calls=%fused_computation.11 | convolution fusion | flops 7252180992 | bytes 31064064 | tf_op jit(solution)/shard_map/dot_general | solution.py:56
  839.0 0.0 reduce-scatter.3.cloned.1.call-update
  839.0 0.2 reduce-scatter.5.cloned.1.call-start
  839.3 4.4 multiply_convert_fusion
  843.7 0.0 reduce-scatter.5.cloned.1.call-update
  843.7 0.1 copy.66
  843.8 0.1 reshape.52
  844.0 0.0 copy-done
  844.0 0.4 fusion.20
  844.4 2.8 gather_fusion
  847.2 0.1 reshape.55
  847.3 0.1 copy.67
  847.4 30.2 %reduce-scatter.3.cloned.1.call-done = bf16[288,768]{1,0:T(8,128)(2,1)} async-done(((bf16[288,3072]{1,0:T(8,128)(2,1)}), bf16[288,768]{1,0:T(8,128)(2,1)}) %reduce-scatter.3.cloned.1.call-update) | async-done | bytes 442384 | tf_op jit(solution)/shard_map/reduce_scatter | solution.py:57
  877.6 1.1 reshape.38
  878.7 1.2 copy.72
  879.9 4.8 all-to-all-start.1
  884.8 0.1 reshape.66
  884.9 0.1 reshape.70
  884.9 5.3 all-to-all-done.1
  890.3 1.5 gather_fusion.1
  891.8 1.5 gather_fusion.2
  893.3 0.9 add_convert_fusion
  894.2 97.1 %reduce-scatter.5.cloned.1.call-done = bf16[48,3072]{1,0:T(8,128)(2,1)} async-done(((bf16[768,3072]{1,0:T(8,128)(2,1)}), bf16[48,3072]{1,0:T(8,128)(2,1)}) %reduce-scatter.5.cloned.1.call-update) | async-done | bytes 294928 | tf_op jit(solution)/shard_map/reduce_scatter | solution.py:88
  (8 shorter events, 0.1 us)
Async XLA Ops:
  7.2 836.8 %copy-start = (bf16[3072,4]{0,1:T(4,128)(2,1)S(1)}, bf16[3072,4]{0,1:T(4,128)(2,1)}, u32[]{:S(2)}) copy-start(bf16[3072,4]{0,1:T(4,128)(2,1)} %param.10) | copy-start | bytes 73732
  7.2 2.3 copy-start.3
  7.2 3.4 copy-start.1
  7.2 275.8 %all-gather.7.cloned.1.call-start = ((), (), s32[]{:S(2)}) async-start(), calls=%async_computation.6 | async-start | bytes 13369344 | tf_op jit(solution)/shard_map/all_gather | solution.py:46
  7.9 545.8 %all-gather.11.cloned.1.call-start = ((), (), s32[]{:S(2)}) async-start(), calls=%async_computation.8 | async-start | bytes 13369344 | tf_op jit(solution)/shard_map/all_gather | solution.py:48
  8.7 815.8 %all-gather.9.cloned.1.call-start = ((), (), s32[]{:S(2)}) async-start(), calls=%async_computation.7 | async-start | bytes 13369344 | tf_op jit(solution)/shard_map/all_gather | solution.py:47
  9.4 868.2 %reduce-scatter.3.cloned.1.call-start = ((), (), s32[]{:S(2)}) async-start(), calls=%async_computation.4 | async-start | bytes 2211840 | tf_op jit(solution)/shard_map/reduce_scatter | solution.py:57
  39.8 784.7 %copy-start.2 = (bf16[288,3072]{1,0:T(8,128)(2,1)S(1)}, bf16[288,3072]{1,0:T(8,128)(2,1)}, u32[]{:S(2)}) copy-start(bf16[288,3072]{1,0:T(8,128)(2,1)} %reshape.37) | copy-start | bytes 5308420
  839.0 152.2 %reduce-scatter.5.cloned.1.call-start = ((), (), s32[]{:S(2)}) async-start(), calls=%async_computation.5 | async-start | bytes 5013504 | tf_op jit(solution)/shard_map/reduce_scatter | solution.py:88
  879.9 10.3 %all-to-all-start.1 = ((bf16[2,4,36,768]{3,0,2,1:T(2,128)(2,1)}), bf16[2,4,36,768]{3,0,2,1:T(2,128)(2,1)S(1)}, u32[]{:S(2)}, u32[]{:S(2)}) async-start(bf16[2,4,36,768]{3,0,2,1:T(2,128)(2,1)} %copy.72), calls=%async_computation.2 | async-start | bytes 884736 | tf_op jit(solution)/shard_map/all_to_all | solution.py:61
Sparse Core Ops, SparseCore 0:
  9.8 273.1 all-gather.6
  284.8 268.8 all-gather.10
  555.5 268.8 all-gather.8
  839.1 38.4 reduce-scatter.2
  880.6 110.5 reduce-scatter.4
where the time goes:
time: 998 us
  waiting for transfers between devices  909 us (91%)
  matrix products  30.4 us (3%)
  blocking collectives  24.9 us (2%)
  between operations  14 us (1%)
  local copies, waits for them, and re-layouts  12.9 us (1%)
    all_gather x1, waiting for transfers between devices, on_device(): up_piece = lax.all_gather(up_rows, 'dp', axis=0, tiled=True)  271 us
    all_gather x1, waiting for transfers between devices, on_device(): down_piece = lax.all_gather(down_rows, 'dp', axis=0, tiled=True)  260 us
    all_gather x1, waiting for transfers between devices, on_device(): gate_piece = lax.all_gather(gate_rows, 'dp', axis=0, tiled=True)  243 us
    reduce_scatter x1, waiting for transfers between devices, on_device(): lax.psum_scatter(rounded.astype(jnp.float32).astype(jnp.bfloat16), 'dp',...  97.1 us
    reduce_scatter x1, waiting for transfers between devices, on_device(): lax.psum_scatter(partial_out.astype(jnp.bfloat16), 'section', scatter_dim...  30.2 us
    all_to_all x1, blocking collectives, on_device(): lax.all_to_all(outgoing, 'expert', split_axis=1, concat_axis=1, tiled=True)  24.9 us
  transfers between devices with their start and end apart: 6, of which 6 were waited for; matrix products, arithmetic and copies ran while one was open for 3% of the time, Pallas kernels for 0%

commit v1 on v0

--- a/solution.py
+++ b/solution.py
@@ -41,7 +41,10 @@
         "mst,mtd->msd", placing, tokens, preferred_element_type=jnp.float32
     ).astype(jnp.bfloat16)
     outgoing = outgoing.reshape(micro_count, experts, capacity, model_width)
-    arrived = lax.all_to_all(outgoing, "expert", split_axis=1, concat_axis=1, tiled=True)
+    count = lax.axis_size("expert")
+    blocks = jnp.stack(jnp.split(outgoing, count, axis=1), axis=0)
+    blocks = lax.all_to_all(blocks, "expert", split_axis=0, concat_axis=0)
+    arrived = jnp.concatenate(blocks, axis=1)
     rows_all = arrived.reshape(-1, model_width)
     gate_piece = lax.all_gather(gate_rows, "dp", axis=0, tiled=True)
     up_piece = lax.all_gather(up_rows, "dp", axis=0, tiled=True)

time: 998 us -> 1000 us (level)
  no operation moved by 1% of the time
where the time goes in v1:
time: 1000 us; the launch traced here: 999 us
  waiting for transfers between devices  906 us (91%)
  matrix products  30.3 us (3%)
  blocking collectives  24.9 us (2%)
  local copies, waits for them, and re-layouts  14.1 us (1%)
  between operations  14 us (1%)
    all_gather x1, waiting for transfers between devices, on_device(): up_piece = lax.all_gather(up_rows, 'dp', axis=0, tiled=True)  271 us
    all_gather x1, waiting for transfers between devices, on_device(): down_piece = lax.all_gather(down_rows, 'dp', axis=0, tiled=True)  262 us
    all_gather x1, waiting for transfers between devices, on_device(): gate_piece = lax.all_gather(gate_rows, 'dp', axis=0, tiled=True)  239 us
    reduce_scatter x1, waiting for transfers between devices, on_device(): lax.psum_scatter(rounded.astype(jnp.float32).astype(jnp.bfloat16), 'dp',...  96.9 us
    reduce_scatter x1, waiting for transfers between devices, on_device(): lax.psum_scatter(partial_out.astype(jnp.bfloat16), 'section', scatter_dim...  30.5 us
    all_to_all x1, blocking collectives, on_device(): blocks = lax.all_to_all(blocks, 'expert', split_axis=0, concat_axis=0)  24.9 us
  transfers between devices with their start and end apart: 6, of which 6 were waited for; matrix products, arithmetic and copies ran while one was open for 3% of the time, Pallas kernels for 0%

profile of v1, /device:TPU:50, one launch (start us, length us, event | category | flops | bytes accessed | tf_op | source)
XLA Modules:
  0.0 999.5 jit_solution(87970168178617235)
XLA Ops:
  7.2 0.0 copy-start
  7.2 0.0 copy-start.3
  7.2 0.0 copy-start.1
  7.2 0.0 all-gather.7.cloned.1.call-start
  7.2 0.7 all-gather.7.cloned.1.call-update
  7.9 0.0 all-gather.11.cloned.1.call-start
  8.0 0.7 all-gather.11.cloned.1.call-update
  8.7 0.0 all-gather.9.cloned.1.call-start
  8.7 0.7 all-gather.9.cloned.1.call-update
  9.4 0.0 reduce-scatter.3.cloned.1.call-start
  9.5 0.0 copy-done.3
  9.5 0.1 copy.71
  9.6 0.1 eq.30
  9.7 0.1 fusion.18
  9.8 0.2 reduce_window_sum.11
  10.0 0.2 select_reduce_fusion
  10.2 0.1 reshape.35
  10.4 0.1 copy.72
  10.5 0.1 convert_reduce_fusion
  10.6 0.0 copy-done.1
  10.6 0.7 convolution_convert_fusion
  11.2 1.8 copy.73
  13.1 1.2 slice_bitcast_fusion.3
  14.3 3.3 pad_maximum_fusion
  17.6 24.9 %all_to_all.10 = bf16[4,2,1,36,3072]{4,1,3,2,0:T(2,128)(2,1)S(1)} all-to-all(bf16[4,2,1,36,3072]{4,1,3,2,0:T(2,128)(2,1)S(1)} %pad_maximum_fusion), channel_id=1, replica_groups=mesh['section'=4,'expert'=4,'dp'=16] {'expert'}, dimensions={0} | all-to-all | bytes 3538944 | tf_op jit(solution)/shard_map/all_to_all | solution.py:46
  42.5 0.4 copy.74
  42.9 1.4 reshape_reshape.3
  44.3 0.0 copy-start.2
  44.3 238.7 %all-gather.7.cloned.1.call-done = bf16[1,2048,3072]{2,1,0:T(8,128)(2,1)} async-done(((bf16[1,128,3072]{2,1,0:T(8,128)(2,1)}), bf16[1,2048,3072]{2,1,0:T(8,128)(2,1)}) %all-gather.7.cloned.1.call-update) | async-done | bytes 12582928 | tf_op jit(solution)/shard_map/all_gather | solution.py:49
  283.0 10.4 %fusion.4 = f32[288,2048]{1,0:T(8,128)} fusion(bf16[288,3072]{1,0:T(8,128)(2,1)} %reshape_reshape.3, bf16[1,2048,3072]{2,1,0:T(8,128)(2,1)} %all-gather.7.cloned.1.call-done), kind=kOutput, calls=%fused_computation.7 | convolution fusion | flops 3623878656 | bytes 16711680 | tf_op jit(solution)/shard_map/dot_general | solution.py:52
  293.4 262.2 %all-gather.11.cloned.1.call-done = bf16[1,2048,3072]{2,1,0:T(8,128)(2,1)} async-done(((bf16[1,128,3072]{2,1,0:T(8,128)(2,1)}), bf16[1,2048,3072]{2,1,0:T(8,128)(2,1)}) %all-gather.11.cloned.1.call-update) | async-done | bytes 12582928 | tf_op jit(solution)/shard_map/all_gather | solution.py:51
  555.6 270.7 %all-gather.9.cloned.1.call-done = bf16[1,2048,3072]{2,1,0:T(8,128)(2,1)} async-done(((bf16[1,128,3072]{2,1,0:T(8,128)(2,1)}), bf16[1,2048,3072]{2,1,0:T(8,128)(2,1)}) %all-gather.9.cloned.1.call-update) | async-done | bytes 12582928 | tf_op jit(solution)/shard_map/all_gather | solution.py:50
  826.3 0.0 copy-done.2
  826.3 14.5 %fusion.6 = bf16[288,3072]{1,0:T(8,128)(2,1)} fusion(bf16[1,2048,3072]{2,1,0:T(8,128)(2,1)} %all-gather.11.cloned.1.call-done, bf16[288,3072]{1,0:T(8,128)(2,1)S(1)} %copy-done.2, bf16[1,2048,3072]{2,1,0:T(8,128)(2,1)} %all-gather.9.cloned.1.call-done, f32[288,2048]{1,0:T(8,128)} %fusion.4), kind=kOutput, calls=%fused_computation.11 | convolution fusion | flops 7252180992 | bytes 31064064 | tf_op jit(solution)/shard_map/dot_general | solution.py:59
  840.8 0.0 reduce-scatter.3.cloned.1.call-update
  840.9 0.0 reduce-scatter.5.cloned.1.call-start
  840.9 4.4 multiply_convert_fusion
  845.3 0.0 reduce-scatter.5.cloned.1.call-update
  845.3 0.1 copy.69
  845.4 0.1 reshape.52
  845.6 0.0 copy-done
  845.6 0.4 fusion.20
  846.0 2.8 gather_fusion
  848.8 0.1 reshape.55
  848.9 0.1 copy.70
  849.1 30.5 %reduce-scatter.3.cloned.1.call-done = bf16[288,768]{1,0:T(8,128)(2,1)} async-done(((bf16[288,3072]{1,0:T(8,128)(2,1)}), bf16[288,768]{1,0:T(8,128)(2,1)}) %reduce-scatter.3.cloned.1.call-update) | async-done | bytes 442384 | tf_op jit(solution)/shard_map/reduce_scatter | solution.py:60
  879.5 1.1 reshape.38
  880.6 1.2 copy.75
  881.9 4.8 all-to-all-start.1
  886.7 0.1 reshape.66
  886.8 0.1 reshape.70
  886.9 5.3 all-to-all-done.1
  892.2 1.5 gather_fusion.1
  893.7 1.5 gather_fusion.2
  895.2 0.9 add_convert_fusion
  896.0 96.9 %reduce-scatter.5.cloned.1.call-done = bf16[48,3072]{1,0:T(8,128)(2,1)} async-done(((bf16[768,3072]{1,0:T(8,128)(2,1)}), bf16[48,3072]{1,0:T(8,128)(2,1)}) %reduce-scatter.5.cloned.1.call-update) | async-done | bytes 294928 | tf_op jit(solution)/shard_map/reduce_scatter | solution.py:91
  (8 shorter events, 0.1 us)
Async XLA Ops:
  7.2 838.4 %copy-start = (bf16[3072,4]{0,1:T(4,128)(2,1)S(1)}, bf16[3072,4]{0,1:T(4,128)(2,1)}, u32[]{:S(2)}) copy-start(bf16[3072,4]{0,1:T(4,128)(2,1)} %param.10) | copy-start | bytes 73732
  7.2 2.3 copy-start.3
  7.2 3.4 copy-start.1
  7.2 275.8 %all-gather.7.cloned.1.call-start = ((), (), s32[]{:S(2)}) async-start(), calls=%async_computation.6 | async-start | bytes 13369344 | tf_op jit(solution)/shard_map/all_gather | solution.py:49
  7.9 547.6 %all-gather.11.cloned.1.call-start = ((), (), s32[]{:S(2)}) async-start(), calls=%async_computation.8 | async-start | bytes 13369344 | tf_op jit(solution)/shard_map/all_gather | solution.py:51
  8.7 817.6 %all-gather.9.cloned.1.call-start = ((), (), s32[]{:S(2)}) async-start(), calls=%async_computation.7 | async-start | bytes 13369344 | tf_op jit(solution)/shard_map/all_gather | solution.py:50
  9.4 870.1 %reduce-scatter.3.cloned.1.call-start = ((), (), s32[]{:S(2)}) async-start(), calls=%async_computation.4 | async-start | bytes 2211840 | tf_op jit(solution)/shard_map/reduce_scatter | solution.py:60
  44.3 781.9 %copy-start.2 = (bf16[288,3072]{1,0:T(8,128)(2,1)S(1)}, bf16[288,3072]{1,0:T(8,128)(2,1)}, u32[]{:S(2)}) copy-start(bf16[288,3072]{1,0:T(8,128)(2,1)} %reshape_reshape.3) | copy-start | bytes 5308420
  840.9 152.1 %reduce-scatter.5.cloned.1.call-start = ((), (), s32[]{:S(2)}) async-start(), calls=%async_computation.5 | async-start | bytes 5013504 | tf_op jit(solution)/shard_map/reduce_scatter | solution.py:91
  881.9 10.3 %all-to-all-start.1 = ((bf16[2,4,36,768]{3,0,2,1:T(2,128)(2,1)}), bf16[2,4,36,768]{3,0,2,1:T(2,128)(2,1)S(1)}, u32[]{:S(2)}, u32[]{:S(2)}) async-start(bf16[2,4,36,768]{3,0,2,1:T(2,128)(2,1)} %copy.75), calls=%async_computation.2 | async-start | bytes 884736 | tf_op jit(solution)/shard_map/all_to_all | solution.py:64
Sparse Core Ops, SparseCore 0:
  9.8 273.1 all-gather.6
  284.8 270.7 all-gather.10
  557.4 268.8 all-gather.8
  841.0 38.4 reduce-scatter.2
  882.5 110.3 reduce-scatter.4
